TPU v7x, 512 devices: a whole 4x4x16 slice. The times are simulated.
512 devices in a mesh: ctx: 64 (over z, y), tp: 8 (over x, core).
Axes of the slice: x: 4, y: 4, z: 16, core: 2. Of those that a mesh axis runs over, the one named last changes fastest.
Arguments:
- features: bfloat16 [3, 4096, 8192], P(None, 'ctx', 'tp'), may hold values from -6 to 6
- short_weight: float32 [3, 3, 8192], P(None, None, 'tp'), may hold values from -3 to 3
- decay_rate: float32 [512, 16], P('tp'), may hold values from 0.00012207031 to 0.03
- residue: float32 [512, 16], P('tp'), may hold values from -3 to 3
- skip_gain: float32 [8192], P('tp'), may hold values from -1 to 1
- out_weight: bfloat16 [8192, 4096], P('tp', 'ctx'), may hold values from -0.1875 to 0.1875
Outputs:
- mixed_out: bfloat16 [4096, 4096], P('ctx', 'tp')
All inputs are finite; a program needn't handle non-finite values.
Results may differ from a plain program's by a relative error of at most 0.006.
Values may be sent and summed in bfloat16 or wider, within the bound.
No kernel may reach another device: no remote copies, remote signals or barrier semaphores. Data moves between devices by JAX's collectives and lax.ppermute only.
A program may use at most 128 MiB of HBM per device.

v0:
```python
import math
import jax
import jax.numpy as jnp
from jax import lax
from jax.sharding import PartitionSpec as P


def passed_along(shard, axis, by):
    length = lax.axis_size(axis)
    pairs = [(i, i + by) for i in range(length) if 0 <= i + by < length]
    return lax.ppermute(shard, axis, pairs)


def entering(value, axis, join, neutral):
    count, mine = (lax.axis_size(axis), lax.axis_index(axis))
    pieces = jax.tree.map(lambda part: lax.all_gather(part, axis), value)
    running = jax.tree.map(
        lambda part, zero: jnp.full_like(part, 0) + jnp.asarray(zero, part.dtype), value, neutral
    )

    def hop(position, running):
        longer = join(running, jax.tree.map(lambda part: part[position], pieces))
        return jax.tree.map(lambda new, old: jnp.where(position < mine, new, old), longer, running)

    return lax.fori_loop(0, count - 1, hop, running)


def combine_states(earlier, later):
    return (earlier[0] * later[0], later[1] + later[0][:, None, :] * earlier[1])


def per_device(features, short_weight, decay_rate, residue, skip_gain, out_weight):
    hi = lax.Precision.HIGHEST
    rows = features.shape[1]
    chans = features.shape[2]
    groups = decay_rate.shape[0]
    modes = decay_rate.shape[1]
    width = chans // groups
    taps = short_weight.shape[1]
    rim = passed_along(features[:, rows - (taps - 1) :, :], "ctx", 1)
    extended = jnp.concatenate([rim, features], axis=1)
    conv = jnp.zeros(features.shape, jnp.float32)
    for j in range(taps):
        conv = conv + short_weight[:, j][:, None, :] * extended[
            :, taps - 1 - j : taps - 1 - j + rows, :
        ].astype(jnp.float32)
    q_lane = conv[0]
    gated = (conv[1] * conv[2]).astype(jnp.bfloat16)
    coef = residue * jnp.sqrt(-jnp.expm1(-2.0 * decay_rate))
    lags = jnp.arange(rows, dtype=jnp.float32)
    near_filter = jnp.sum(
        coef[:, :, None] * jnp.exp(-decay_rate[:, :, None] * lags[None, None, :]), axis=1
    ).astype(jnp.bfloat16)
    index = jnp.arange(rows, dtype=jnp.int32)
    offset = index[:, None] - index[None, :]
    lower = offset >= 0
    clipped = jnp.clip(offset, 0, rows - 1)
    gstep = math.gcd(groups, 8)
    nblock = groups // gstep
    filter_blocks = near_filter.reshape(nblock, gstep, rows)
    input_blocks = gated.reshape(rows, nblock, gstep, width).transpose(1, 0, 2, 3)

    def near_block(pair):
        taps_here, inputs_here = pair
        toeplitz = jnp.where(lower[None], taps_here[:, clipped], jnp.zeros((), jnp.bfloat16))
        return jnp.einsum("gts,sgw->tgw", toeplitz, inputs_here, preferred_element_type=jnp.float32)

    near = (
        lax.map(near_block, (filter_blocks, input_blocks))
        .transpose(1, 0, 2, 3)
        .reshape(rows, chans)
    )
    gated_wide = gated.astype(jnp.float32)
    grouped = gated_wide.reshape(rows, groups, width)
    end_basis = jnp.exp(-decay_rate[None] * (rows - 1.0 - lags)[:, None, None])
    own_state = jnp.einsum("tgs,tgw->gws", end_basis, grouped, precision=hi)
    block_decay = jnp.exp(-decay_rate * rows)
    identity = (
        jnp.ones((groups, modes), jnp.float32),
        jnp.zeros((groups, width, modes), jnp.float32),
    )
    incoming = entering((block_decay, own_state), "ctx", combine_states, identity)[1]
    far_basis = coef[None] * jnp.exp(-decay_rate[None] * (lags + 1.0)[:, None, None])
    far = jnp.einsum("tgs,gws->tgw", far_basis, incoming, precision=hi).reshape(rows, chans)
    mixed = (q_lane * (near + far + skip_gain[None, :] * gated_wide)).astype(jnp.bfloat16)
    partial_out = jnp.dot(
        mixed,
        lax.all_gather(out_weight, "ctx", axis=1, tiled=True),
        preferred_element_type=jnp.float32,
    )
    return lax.psum_scatter(partial_out, "tp", scatter_dimension=1, tiled=True).astype(jnp.bfloat16)


def solution(mesh):
    placed = (
        P(None, "ctx", "tp"),
        P(None, None, "tp"),
        P("tp", None),
        P("tp", None),
        P("tp"),
        P("tp", "ctx"),
    )
    return jax.shard_map(
        per_device, mesh=mesh, in_specs=placed, out_specs=P("ctx", "tp"), check_vma=False
    )
```

profile of v0, /device:TPU:8, one launch (start us, length us, event | category | flops | bytes accessed | tf_op | source)
XLA Modules:
  0.0 521.5 jit_solution(11579085921228791961)
XLA Ops:
  7.4 3.5 collective-permute-start
  12.6 1.4 copy.41
  14.0 2.1 collective-permute-done
  16.5 2.2 multiply_add_fusion
  18.7 1.4 fusion.23
  21.1 113.2 %all-gather.2 = f32[64,64,16]{1,2,0:T(8,128)} all-gather(f32[1,64,16]{1,2,0:T(8,128)S(1)} %get-tuple-element.216), channel_id=3, replica_groups=mesh['ctx'=64,'tp'=8] {'ctx'}, dimensions={0}, use_global_device_ids=true | all-gather | bytes 266240 | tf_op jit(solution)/shard_map/all_gather | solution.py:16
  134.7 108.6 %while.25 = (s32[]{:T(128)}, f32[8,64,8,16]{1,3,2,0:T(8,128)}, bf16[8,64,8,16]{1,3,2,0:T(8,128)(2,1)S(1)}, bf16[8,8,64]{2,1,0:T(8,128)(2,1)S(1)}, s32[]{:T(128)}) while((s32[]{:T(128)}, f32[8,64,8,16]{1,3,2,0:T(8,128)}, bf16[8,64,8,16]{1,3,2,0:T(8,128)(2,1)S(1)}, bf16[8,8,64]{2,1,0:T(8,128)(2,1)S(1)}, s32[]{:T(128)}) %tuple.73), condition=%wide.region_2.3_spmd.clone, body=%wide.region_1.2_spmd.clone.sunk | while | flops 1114114 | bytes 607297 | solution.py:69
  134.9 12.1 %gather_fusion = bf16[4096,8]{1,0:T(8,128)(2,1)S(1)} fusion(bf16[8,64]{0,1:T(8,128)(2,1)S(1)} %bitcast.80, s32[4096]{0:T(1024)S(1)} %broadcast_clamp_fusion.2), kind=kCustom, calls=%fused_computation.clone.clone.1 | custom fusion | bytes 147456 | tf_op jit(solution)/shard_map/while/body/eval_jaxpr/gather | solution.py:65
  148.5 12.1 %gather_fusion = bf16[4096,8]{1,0:T(8,128)(2,1)S(1)} fusion(bf16[8,64]{0,1:T(8,128)(2,1)S(1)} %bitcast.80, s32[4096]{0:T(1024)S(1)} %broadcast_clamp_fusion.2), kind=kCustom, calls=%fused_computation.clone.clone.1 | custom fusion | bytes 147456 | tf_op jit(solution)/shard_map/while/body/eval_jaxpr/gather | solution.py:65
  162.0 12.1 %gather_fusion = bf16[4096,8]{1,0:T(8,128)(2,1)S(1)} fusion(bf16[8,64]{0,1:T(8,128)(2,1)S(1)} %bitcast.80, s32[4096]{0:T(1024)S(1)} %broadcast_clamp_fusion.2), kind=kCustom, calls=%fused_computation.clone.clone.1 | custom fusion | bytes 147456 | tf_op jit(solution)/shard_map/while/body/eval_jaxpr/gather | solution.py:65
  175.6 12.1 %gather_fusion = bf16[4096,8]{1,0:T(8,128)(2,1)S(1)} fusion(bf16[8,64]{0,1:T(8,128)(2,1)S(1)} %bitcast.80, s32[4096]{0:T(1024)S(1)} %broadcast_clamp_fusion.2), kind=kCustom, calls=%fused_computation.clone.clone.1 | custom fusion | bytes 147456 | tf_op jit(solution)/shard_map/while/body/eval_jaxpr/gather | solution.py:65
  189.2 12.1 %gather_fusion = bf16[4096,8]{1,0:T(8,128)(2,1)S(1)} fusion(bf16[8,64]{0,1:T(8,128)(2,1)S(1)} %bitcast.80, s32[4096]{0:T(1024)S(1)} %broadcast_clamp_fusion.2), kind=kCustom, calls=%fused_computation.clone.clone.1 | custom fusion | bytes 147456 | tf_op jit(solution)/shard_map/while/body/eval_jaxpr/gather | solution.py:65
  202.8 12.1 %gather_fusion = bf16[4096,8]{1,0:T(8,128)(2,1)S(1)} fusion(bf16[8,64]{0,1:T(8,128)(2,1)S(1)} %bitcast.80, s32[4096]{0:T(1024)S(1)} %broadcast_clamp_fusion.2), kind=kCustom, calls=%fused_computation.clone.clone.1 | custom fusion | bytes 147456 | tf_op jit(solution)/shard_map/while/body/eval_jaxpr/gather | solution.py:65
  216.3 12.1 %gather_fusion = bf16[4096,8]{1,0:T(8,128)(2,1)S(1)} fusion(bf16[8,64]{0,1:T(8,128)(2,1)S(1)} %bitcast.80, s32[4096]{0:T(1024)S(1)} %broadcast_clamp_fusion.2), kind=kCustom, calls=%fused_computation.clone.clone.1 | custom fusion | bytes 147456 | tf_op jit(solution)/shard_map/while/body/eval_jaxpr/gather | solution.py:65
  229.9 12.1 %gather_fusion = bf16[4096,8]{1,0:T(8,128)(2,1)S(1)} fusion(bf16[8,64]{0,1:T(8,128)(2,1)S(1)} %bitcast.80, s32[4096]{0:T(1024)S(1)} %broadcast_clamp_fusion.2), kind=kCustom, calls=%fused_computation.clone.clone.1 | custom fusion | bytes 147456 | tf_op jit(solution)/shard_map/while/body/eval_jaxpr/gather | solution.py:65
  243.3 71.3 %all-gather.8.cloned.1.call-done = f32[4096,16,16]{2,1,0:T(8,128)} async-done(((f32[64,16,16]{2,1,0:T(8,128)}), f32[4096,16,16]{2,1,0:T(8,128)}) %all-gather.8.cloned.1.call-update) | async-done | bytes 4194320 | tf_op jit(solution)/shard_map/all_gather | solution.py:16
  314.6 22.6 %copy.48 = f32[64,64,16,16]{1,3,2,0:T(8,128)} copy(f32[64,64,16,16]{3,2,1,0:T(8,128)} %bitcast.81) | data formatting | bytes 8388608
  337.2 106.0 %while.26 = (s32[]{:T(128)}, f32[64,16,16]{0,2,1:T(8,128)S(1)}, s32[]{:T(128)}, f32[64,64,16,16]{1,3,2,0:T(8,128)}, f32[64,64,16]{1,2,0:T(8,128)}, /*index=5*/s32[]{:T(128)}, s32[]{:T(128)}) while((s32[]{:T(128)}, f32[64,16,16]{0,2,1:T(8,128)S(1)}, s32[]{:T(128)}, f32[64,64,16,16]{1,3,2,0:T(8,128)}, f32[64,64,16]{1,2,0:T(8,128)}, ...), condition=%wide.region_4.5_spmd.clone, body=%wide.region_3.4_spmd.clone.sunk | while | flops 65540 | bytes 209001 | solution.py:25
  401.8 1.0 fusion.46
  410.2 1.0 fusion.46
  444.5 25.6 %all-gather.6.cloned.1.call-done = bf16[1024,4096]{0,1:T(8,128)(2,1)} async-done(((bf16[1024,64]{0,1:T(8,128)(2,1)}), bf16[1024,4096]{0,1:T(8,128)(2,1)}) %all-gather.6.cloned.1.call-update) | async-done | bytes 8388624 | tf_op jit(solution)/shard_map/all_gather | solution.py:88
  470.1 7.0 %fusion.32 = f32[64,4096]{1,0:T(8,128)} fusion(bf16[64,1024]{0,1:T(8,128)(2,1)S(1)} %fusion.17, bf16[1024,4096]{0,1:T(8,128)(2,1)} %all-gather.6.cloned.1.call-done), kind=kOutput, calls=%fused_computation.53 | convolution fusion | flops 536870912 | bytes 9568256 | tf_op jit(solution)/shard_map/dot_general | solution.py:86
  477.2 36.2 %reduce-scatter.2.cloned.1.call-done = f32[64,512]{1,0:T(8,128)} async-done(((f32[64,4096]{1,0:T(8,128)}), f32[64,512]{1,0:T(8,128)}) %reduce-scatter.2.cloned.1.call-update) | async-done | bytes 131088 | tf_op jit(solution)/shard_map/reduce_scatter | solution.py:91
  513.4 1.5 convert_element_type.51
  (215 shorter events, 120.0 us)
Async XLA Ops:
  6.5 308.0 %all-gather.8.cloned.1.call-start = ((), (), s32[]{:S(2)}) async-start(), calls=%async_computation.3 | async-start | bytes 34078720 | tf_op jit(solution)/shard_map/all_gather | solution.py:16
  7.4 8.7 %collective-permute-start = (bf16[3,2,1024]{2,1,0:T(2,128)(2,1)S(1)}, bf16[3,2,1024]{2,1,0:T(2,128)(2,1)S(1)}, u32[]{:S(2)}, u32[]{:S(2)}) collective-permute-start(bf16[3,2,1024]{2,1,0:T(2,128)(2,1)S(1)} %slice.29), channel_id=1, source_target_pairs={{0,8},{8,16},{16,24},{24,32},{32,40},{40,48},{48,56},{56,64},{64,7... | collective-permute-start | bytes 36872 | tf_op jit(solution)/shard_map/ppermute | solution.py:11
  20.2 449.9 %all-gather.6.cloned.1.call-start = ((), (), s32[]{:S(2)}) async-start(), calls=%async_computation.1 | async-start | bytes 8519680 | tf_op jit(solution)/shard_map/all_gather | solution.py:88
  21.0 492.4 %reduce-scatter.2.cloned.1.call-start = ((), (), s32[]{:S(2)}) async-start(), calls=%async_computation.2 | async-start | bytes 1179648 | tf_op jit(solution)/shard_map/reduce_scatter | solution.py:91
  337.2 107.1 %copy-start = (f32[8,64,8,16]{1,3,2,0:T(8,128)S(1)}, f32[8,64,8,16]{1,3,2,0:T(8,128)}, u32[]{:S(2)}) copy-start(f32[8,64,8,16]{1,3,2,0:T(8,128)} %get-tuple-element.131) | copy-start | bytes 786436
  337.2 107.1 %copy-start.1 = (f32[1024]{0:T(1024)S(1)}, f32[1024]{0:T(1024)}, u32[]{:S(2)}) copy-start(f32[1024]{0:T(1024)} %param.14) | copy-start | bytes 12292
Sparse Core Ops, SparseCore 0:
  20.3 294.1 all-gather.7
  317.5 152.5 all-gather.5
  477.3 36.0 reduce-scatter.1
where the time goes:
time: 526 us; the launch traced here: 521 us
  local copies, waits for them, and re-layouts  173 us (33%)
  waiting for transfers between devices  136 us (26%)
  blocking collectives  113 us (21%)
  other arithmetic  65.9 us (13%)
  matrix products  15.8 us (3%)
  between operations  13.2 us (3%)
    all_gather x1, blocking collectives, entering(): pieces = jax.tree.map(lambda part: lax.all_gather(part, axis), value)  113 us
    gather x16, local copies, waits for them, and re-layouts, near_block(): taps_here[:, clipped]  100 us
    all_gather x1, waiting for transfers between devices, entering(): pieces = jax.tree.map(lambda part: lax.all_gather(part, axis), value)  71.3 us
    select_n x63, other arithmetic, hop(): jnp.where(position < mine, new, old)  60.5 us
    mul x63, local copies, waits for them, and re-layouts, combine_states(): return (earlier[0] * later[0], later[1] + later[0][:, None, :] * earlier[1])  44.3 us
    reduce_scatter x1, waiting for transfers between devices, per_device(): lax.psum_scatter(partial_out, 'tp', scatter_dimension=1, tiled=True)  36.2 us
    all_gather x1, waiting for transfers between devices, per_device(): lax.all_gather(out_weight, 'ctx', axis=1, tiled=True)  25.6 us
    unnamed x8, local copies, waits for them, and re-layouts  24 us
  transfers between devices with their start and end apart: 4, of which 4 were waited for; matrix products, arithmetic and copies ran while one was open for 46% of the time, Pallas kernels for 0%

commit v1 on v0

--- a/solution.py
+++ b/solution.py
@@ -1,8 +1,24 @@
+import functools
 import math
 import jax
 import jax.numpy as jnp
 from jax import lax
 from jax.sharding import PartitionSpec as P
+
+
+def carry_blocks_here(vec, comm_axis):
+    return jnp.concatenate(
+        lax.all_to_all(
+            jnp.stack(tuple((vec for _ in range(lax.axis_size(comm_axis))))),
+            axis_name=comm_axis,
+            split_axis=0,
+            concat_axis=0,
+        ),
+        axis=1,
+    )
+
+
+plan_the_trails = functools.partial(carry_blocks_here, comm_axis="ctx")
 
 
 def passed_along(shard, axis, by):
@@ -83,11 +99,7 @@
     far_basis = coef[None] * jnp.exp(-decay_rate[None] * (lags + 1.0)[:, None, None])
     far = jnp.einsum("tgs,gws->tgw", far_basis, incoming, precision=hi).reshape(rows, chans)
     mixed = (q_lane * (near + far + skip_gain[None, :] * gated_wide)).astype(jnp.bfloat16)
-    partial_out = jnp.dot(
-        mixed,
-        lax.all_gather(out_weight, "ctx", axis=1, tiled=True),
-        preferred_element_type=jnp.float32,
-    )
+    partial_out = jnp.dot(mixed, plan_the_trails(out_weight), preferred_element_type=jnp.float32)
     return lax.psum_scatter(partial_out, "tp", scatter_dimension=1, tiled=True).astype(jnp.bfloat16)
 
 

time: 526 us -> 875 us (1.66)
  blocking collectives: 113 us -> 463 us
  waiting for transfers between devices: 136 us -> 114 us
  starting transfers between devices: 3.57 us -> 22.5 us
    all_gather x1, blocking collectives: 113 us -> 463 us  [entering(): pieces = jax.tree.map(lambda part: lax.all_gather(part, axis), value)]
    all_gather x1 -> x0, waiting for transfers between devices: 25.6 us -> none  [per_device(): lax.all_gather(out_weight, 'ctx', axis=1, tiled=True)]
    all_to_all x0 -> x1, starting transfers between devices: none -> 19.1 us  [carry_blocks_here(): lax.all_to_all(jnp.stack(tuple((vec for _ in range(lax.axis_size(comm_axi...]
    unnamed x8 -> x16, local copies, waits for them, and re-layouts: 24 us -> 23 us
  transfers between devices with their start and end apart: 4 -> 4, of which waited for: 4 -> 3; matrix products, arithmetic and copies ran while one was open for 46% -> 28% of each run, Pallas kernels for 0% -> 0%
where the time goes in v1:
time: 875 us; the launch traced here: 871 us
  blocking collectives  463 us (53%)
  local copies, waits for them, and re-layouts  175 us (20%)
  waiting for transfers between devices  114 us (13%)
  other arithmetic  65.1 us (7%)
  starting transfers between devices  22.5 us (3%)
  matrix products  15.8 us (2%)
  between operations  13.6 us (2%)
    all_gather x1, blocking collectives, entering(): pieces = jax.tree.map(lambda part: lax.all_gather(part, axis), value)  463 us
    gather x16, local copies, waits for them, and re-layouts, near_block(): taps_here[:, clipped]  100 us
    all_gather x1, waiting for transfers between devices, entering(): pieces = jax.tree.map(lambda part: lax.all_gather(part, axis), value)  72.6 us
    select_n x63, other arithmetic, hop(): jnp.where(position < mine, new, old)  60.4 us
    mul x63, local copies, waits for them, and re-layouts, combine_states(): return (earlier[0] * later[0], later[1] + later[0][:, None, :] * earlier[1])  44.3 us
    reduce_scatter x1, waiting for transfers between devices, per_device(): lax.psum_scatter(partial_out, 'tp', scatter_dimension=1, tiled=True)  37.6 us
    unnamed x16, local copies, waits for them, and re-layouts  23 us
    all_to_all x1, starting transfers between devices, carry_blocks_here(): lax.all_to_all(jnp.stack(tuple((vec for _ in range(lax.axis_size(comm_axi...  19.1 us
  transfers between devices with their start and end apart: 4, of which 3 were waited for; matrix products, arithmetic and copies ran while one was open for 28% of the time, Pallas kernels for 0%

profile of v1, /device:TPU:8, one launch (start us, length us, event | category | flops | bytes accessed | tf_op | source)
XLA Modules:
  0.0 870.7 jit_solution(16698755845882060446)
XLA Ops:
  6.5 5.2 stack.2
  11.7 19.1 %all-to-all-start = ((bf16[64,1024,64]{1,2,0:T(8,128)(2,1)}), bf16[64,1024,64]{1,2,0:T(8,128)(2,1)}, u32[]{:S(2)}, u32[]{:S(2)}) async-start(bf16[64,1024,64]{1,2,0:T(8,128)(2,1)} %stack.2), calls=%async_computation | async-start | bytes 16777216 | tf_op jit(solution)/shard_map/all_to_all | solution.py:11
  30.9 3.4 collective-permute-start
  34.9 3.6 collective-permute-done
  38.9 2.2 multiply_add_fusion
  41.1 1.4 fusion.22
  42.8 463.4 %all-gather.2 = f32[64,64,16]{1,2,0:T(8,128)} all-gather(f32[1,64,16]{1,2,0:T(8,128)S(1)} %get-tuple-element.215), channel_id=3, replica_groups=mesh['ctx'=64,'tp'=8] {'ctx'}, dimensions={0}, use_global_device_ids=true | all-gather | bytes 266240 | tf_op jit(solution)/shard_map/all_gather | solution.py:32
  506.6 108.6 %while.25 = (s32[]{:T(128)}, f32[8,64,8,16]{1,3,2,0:T(8,128)}, bf16[8,64,8,16]{1,3,2,0:T(8,128)(2,1)S(1)}, bf16[8,8,64]{2,1,0:T(8,128)(2,1)S(1)}, s32[]{:T(128)}) while((s32[]{:T(128)}, f32[8,64,8,16]{1,3,2,0:T(8,128)}, bf16[8,64,8,16]{1,3,2,0:T(8,128)(2,1)S(1)}, bf16[8,8,64]{2,1,0:T(8,128)(2,1)S(1)}, s32[]{:T(128)}) %tuple.71), condition=%wide.region_2.3_spmd.clone, body=%wide.region_1.2_spmd.clone.sunk | while | flops 1114114 | bytes 607297 | solution.py:85
  506.8 12.1 %gather_fusion = bf16[4096,8]{1,0:T(8,128)(2,1)S(1)} fusion(bf16[8,64]{0,1:T(8,128)(2,1)S(1)} %bitcast.77, s32[4096]{0:T(1024)S(1)} %broadcast_clamp_fusion.2), kind=kCustom, calls=%fused_computation.clone.clone.1 | custom fusion | bytes 147456 | tf_op jit(solution)/shard_map/while/body/eval_jaxpr/gather | solution.py:81
  520.4 12.1 %gather_fusion = bf16[4096,8]{1,0:T(8,128)(2,1)S(1)} fusion(bf16[8,64]{0,1:T(8,128)(2,1)S(1)} %bitcast.77, s32[4096]{0:T(1024)S(1)} %broadcast_clamp_fusion.2), kind=kCustom, calls=%fused_computation.clone.clone.1 | custom fusion | bytes 147456 | tf_op jit(solution)/shard_map/while/body/eval_jaxpr/gather | solution.py:81
  534.0 12.1 %gather_fusion = bf16[4096,8]{1,0:T(8,128)(2,1)S(1)} fusion(bf16[8,64]{0,1:T(8,128)(2,1)S(1)} %bitcast.77, s32[4096]{0:T(1024)S(1)} %broadcast_clamp_fusion.2), kind=kCustom, calls=%fused_computation.clone.clone.1 | custom fusion | bytes 147456 | tf_op jit(solution)/shard_map/while/body/eval_jaxpr/gather | solution.py:81
  547.5 12.1 %gather_fusion = bf16[4096,8]{1,0:T(8,128)(2,1)S(1)} fusion(bf16[8,64]{0,1:T(8,128)(2,1)S(1)} %bitcast.77, s32[4096]{0:T(1024)S(1)} %broadcast_clamp_fusion.2), kind=kCustom, calls=%fused_computation.clone.clone.1 | custom fusion | bytes 147456 | tf_op jit(solution)/shard_map/while/body/eval_jaxpr/gather | solution.py:81
  561.1 12.1 %gather_fusion = bf16[4096,8]{1,0:T(8,128)(2,1)S(1)} fusion(bf16[8,64]{0,1:T(8,128)(2,1)S(1)} %bitcast.77, s32[4096]{0:T(1024)S(1)} %broadcast_clamp_fusion.2), kind=kCustom, calls=%fused_computation.clone.clone.1 | custom fusion | bytes 147456 | tf_op jit(solution)/shard_map/while/body/eval_jaxpr/gather | solution.py:81
  574.7 12.1 %gather_fusion = bf16[4096,8]{1,0:T(8,128)(2,1)S(1)} fusion(bf16[8,64]{0,1:T(8,128)(2,1)S(1)} %bitcast.77, s32[4096]{0:T(1024)S(1)} %broadcast_clamp_fusion.2), kind=kCustom, calls=%fused_computation.clone.clone.1 | custom fusion | bytes 147456 | tf_op jit(solution)/shard_map/while/body/eval_jaxpr/gather | solution.py:81
  588.3 12.1 %gather_fusion = bf16[4096,8]{1,0:T(8,128)(2,1)S(1)} fusion(bf16[8,64]{0,1:T(8,128)(2,1)S(1)} %bitcast.77, s32[4096]{0:T(1024)S(1)} %broadcast_clamp_fusion.2), kind=kCustom, calls=%fused_computation.clone.clone.1 | custom fusion | bytes 147456 | tf_op jit(solution)/shard_map/while/body/eval_jaxpr/gather | solution.py:81
  601.8 12.1 %gather_fusion = bf16[4096,8]{1,0:T(8,128)(2,1)S(1)} fusion(bf16[8,64]{0,1:T(8,128)(2,1)S(1)} %bitcast.77, s32[4096]{0:T(1024)S(1)} %broadcast_clamp_fusion.2), kind=kCustom, calls=%fused_computation.clone.clone.1 | custom fusion | bytes 147456 | tf_op jit(solution)/shard_map/while/body/eval_jaxpr/gather | solution.py:81
  615.2 72.6 %all-gather.5.cloned.1.call-done = f32[4096,16,16]{2,1,0:T(8,128)} async-done(((f32[64,16,16]{2,1,0:T(8,128)}), f32[4096,16,16]{2,1,0:T(8,128)}) %all-gather.5.cloned.1.call-update) | async-done | bytes 4194320 | tf_op jit(solution)/shard_map/all_gather | solution.py:32
  687.8 22.6 %copy.49 = f32[64,64,16,16]{1,3,2,0:T(8,128)} copy(f32[64,64,16,16]{3,2,1,0:T(8,128)} %bitcast.78) | data formatting | bytes 8388608
  710.4 105.8 %while.26 = (s32[]{:T(128)}, f32[64,16,16]{0,2,1:T(8,128)S(1)}, s32[]{:T(128)}, f32[64,64,16,16]{1,3,2,0:T(8,128)}, f32[64,64,16]{1,2,0:T(8,128)}, /*index=5*/s32[]{:T(128)}, s32[]{:T(128)}) while((s32[]{:T(128)}, f32[64,16,16]{0,2,1:T(8,128)S(1)}, s32[]{:T(128)}, f32[64,64,16,16]{1,3,2,0:T(8,128)}, f32[64,64,16]{1,2,0:T(8,128)}, ...), condition=%wide.region_4.5_spmd.clone, body=%wide.region_3.4_spmd.clone.sunk | while | flops 65540 | bytes 209001 | solution.py:41
  711.2 1.0 fusion.45
  714.5 1.0 fusion.45
  817.6 7.0 fusion.25
  824.7 37.6 %reduce-scatter.2.cloned.1.call-done = f32[64,512]{1,0:T(8,128)} async-done(((f32[64,4096]{1,0:T(8,128)}), f32[64,512]{1,0:T(8,128)}) %reduce-scatter.2.cloned.1.call-update) | async-done | bytes 131088 | tf_op jit(solution)/shard_map/reduce_scatter | solution.py:103
  862.4 1.5 convert_element_type.52
  (223 shorter events, 117.2 us)
Async XLA Ops:
  11.7 19.1 %copy-start.1 = (bf16[3,64,1024]{2,1,0:T(8,128)(2,1)S(1)}, bf16[3,64,1024]{2,1,0:T(8,128)(2,1)}, u32[]{:S(2)}) copy-start(bf16[3,64,1024]{2,1,0:T(8,128)(2,1)} %param.10) | copy-start | bytes 1179652
  11.7 22.5 %copy-start.3 = (f32[64,16]{0,1:T(8,128)S(1)}, f32[64,16]{0,1:T(8,128)}, u32[]{:S(2)}) copy-start(f32[64,16]{0,1:T(8,128)} %param.12) | copy-start | bytes 12292
  11.7 22.5 %copy-start.4 = (f32[64,16]{0,1:T(8,128)S(1)}, f32[64,16]{0,1:T(8,128)}, u32[]{:S(2)}) copy-start(f32[64,16]{0,1:T(8,128)} %param.13) | copy-start | bytes 12292
  11.7 22.6 %copy-start.2 = (f32[3,3,1024]{2,1,0:T(4,128)S(1)}, f32[3,3,1024]{2,1,0:T(4,128)}, u32[]{:S(2)}) copy-start(f32[3,3,1024]{2,1,0:T(4,128)} %param.11) | copy-start | bytes 110596
  11.7 805.9 %all-to-all-start = ((bf16[64,1024,64]{1,2,0:T(8,128)(2,1)}), bf16[64,1024,64]{1,2,0:T(8,128)(2,1)}, u32[]{:S(2)}, u32[]{:S(2)}) async-start(bf16[64,1024,64]{1,2,0:T(8,128)(2,1)} %stack.2), calls=%async_computation | async-start | bytes 16777216 | tf_op jit(solution)/shard_map/all_to_all | solution.py:11
  30.8 657.0 %all-gather.5.cloned.1.call-start = ((), (), s32[]{:S(2)}) async-start(), calls=%async_computation.3 | async-start | bytes 34078720 | tf_op jit(solution)/shard_map/all_gather | solution.py:32
  30.9 7.6 collective-permute-start
  42.6 819.8 %reduce-scatter.2.cloned.1.call-start = ((), (), s32[]{:S(2)}) async-start(), calls=%async_computation.2 | async-start | bytes 1179648 | tf_op jit(solution)/shard_map/reduce_scatter | solution.py:103
  710.4 107.0 %copy-start = (f32[8,64,8,16]{1,3,2,0:T(8,128)S(1)}, f32[8,64,8,16]{1,3,2,0:T(8,128)}, u32[]{:S(2)}) copy-start(f32[8,64,8,16]{1,3,2,0:T(8,128)} %get-tuple-element.131) | copy-start | bytes 786436
  710.4 107.0 %copy-start.5 = (f32[1024]{0:T(1024)S(1)}, f32[1024]{0:T(1024)}, u32[]{:S(2)}) copy-start(f32[1024]{0:T(1024)} %param.14) | copy-start | bytes 12292
Sparse Core Ops, SparseCore 0:
  42.7 645.0 all-gather.4
  824.8 37.4 reduce-scatter.1
